TPU v7x, 512 devices: a whole 4x4x16 slice. The times are simulated.
512 devices in a mesh: seq: 128 (over x, z, core), head: 4 (over y).
Axes of the slice: x: 4, y: 4, z: 16, core: 2. Of those that a mesh axis runs over, the one named last changes fastest.
Arguments:
- hidden: bfloat16 [32768, 2560], P(('seq', 'head')), may hold values from -6 to 6
- w_values: bfloat16 [2560, 2560], P('seq', 'head'), may hold values from -0.125 to 0.125
- w_gates: bfloat16 [2560, 2560], P('seq', 'head'), may hold values from -0.125 to 0.125
- w_steps: bfloat16 [2560, 40], P('seq', 'head'), may hold values from -0.0625 to 0.0625
- w_states: bfloat16 [2560, 256], P('seq'), may hold values from -0.125 to 0.125
- conv_weight: float32 [4, 2816], replicated, may hold values from -3 to 3
- conv_bias: float32 [2816], replicated, may hold values from -3 to 3
- step_bias: float32 [40], P('head'), may hold values from -1 to 0.5
- decay_rate: float32 [40], P('head'), may hold values from 0 to 1, as said below
- skip_gain: float32 [40], P('head'), may hold values from 1 to 8
- norm_gain: float32 [2560], replicated, may hold values from 0.5 to 1.5
- lengths: int32 [64], replicated, may hold values from 256 to 768, as said below
Outputs:
- gated_out: bfloat16 [32768, 2560], P(('seq', 'head'))
- final_states: float32 [128, 40, 64, 128], P('seq', 'head')
Inputs may be any that keep to these rules, and one draw needn't show every extreme that they name: Prompts are packed in order, each holding 256 to 768 tokens; the lengths sum to 32768. `decay_rate`: positive rates.
All inputs are finite; a program needn't handle non-finite values.
Results may differ from a plain program's by a relative error of at most 0.01.
Values may be sent and summed in bfloat16 or wider, within the bound.
No kernel may reach another device: no remote copies, remote signals or barrier semaphores. Data moves between devices by JAX's collectives and lax.ppermute only.
A program may use at most 128 MiB of HBM per device.

v0:
```python
import jax
import jax.numpy as jnp
from jax import lax
from jax.sharding import PartitionSpec as P

STRETCH = 256
epsilon = 1e-05


def from_behind(block, axis, distance):
    devices = range(lax.axis_size(axis))
    route = [(i - distance, i) for i in devices if i - distance in devices]
    return lax.ppermute(block, axis, route)


def segments_at(positions, prompt_ends):
    counted = jnp.sum((prompt_ends[None, :] <= positions[:, None]).astype(jnp.int32), axis=1)
    return jnp.where(positions < 0, -1, counted)


def on_device(
    hidden,
    w_values,
    w_gates,
    w_steps,
    w_states,
    conv_weight,
    conv_bias,
    step_bias,
    decay_rate,
    skip_gain,
    norm_gain,
    lengths,
):
    groups = lax.axis_size("head")
    group_index = lax.axis_index("head")
    block_index = lax.axis_index("seq")
    local_width = w_values.shape[1]
    inner_width = local_width * groups
    local_heads = decay_rate.shape[0]
    head_width = local_width // local_heads
    state_width = w_states.shape[1] // 2
    conv_taps = conv_weight.shape[0]
    prompt_ends = jnp.cumsum(lengths)
    block_hidden = lax.all_to_all(
        jnp.broadcast_to(hidden[None], (groups,) + hidden.shape), "head", 0, 0, tiled=True
    ).reshape(groups * hidden.shape[0], hidden.shape[1])
    block_rows = block_hidden.shape[0]
    sub_rows = block_rows // groups
    step_width = w_steps.shape[1]
    merged = jnp.concatenate([w_values, w_states, w_gates, w_steps], axis=1)
    full = lax.all_gather(merged, "seq", axis=0, tiled=True)
    projected = jnp.dot(block_hidden, full, preferred_element_type=jnp.float32)
    conv_end = local_width + 2 * state_width
    pre_rows = projected[:, :conv_end].astype(jnp.bfloat16)
    gates_sum = projected[:, conv_end : conv_end + local_width]
    steps_sum = projected[:, conv_end + local_width : conv_end + local_width + step_width]
    local_taps = jnp.concatenate(
        [
            lax.dynamic_slice_in_dim(conv_weight, group_index * local_width, local_width, 1),
            conv_weight[:, inner_width:],
        ],
        axis=1,
    )
    local_bias = jnp.concatenate(
        [
            lax.dynamic_slice_in_dim(conv_bias, group_index * local_width, local_width, 0),
            conv_bias[inner_width:],
        ],
        axis=0,
    )
    block_start = block_index * block_rows
    rim_rows = pre_rows[block_rows - (conv_taps - 1) :]
    prior_rim = from_behind(rim_rows, "seq", 1)
    extended = jnp.concatenate([prior_rim, pre_rows], axis=0)
    ext_positions = (
        block_start - (conv_taps - 1) + jnp.arange(block_rows + conv_taps - 1, dtype=jnp.int32)
    )
    ext_ids = segments_at(ext_positions, prompt_ends)
    own_ids = ext_ids[conv_taps - 1 :]
    filtered = jnp.zeros(pre_rows.shape, jnp.float32) + local_bias[None, :]
    for offset in range(conv_taps):
        matches = (ext_ids[offset : offset + block_rows] == own_ids).astype(jnp.float32)
        filtered = (
            filtered
            + local_taps[offset][None, :]
            * extended[offset : offset + block_rows].astype(jnp.float32)
            * matches[:, None]
        )
    conv_out = jax.nn.silu(filtered).astype(jnp.bfloat16)
    head_values = conv_out[:, :local_width]
    both_states = conv_out[:, local_width:]
    stretch_rows = STRETCH
    stretches = block_rows // stretch_rows
    positions = block_start + jnp.arange(block_rows, dtype=jnp.int32)
    segment_ids = segments_at(positions, prompt_ends)
    next_ids = segments_at(positions + 1, prompt_ends)
    before_ids = segments_at(positions - 1, prompt_ends)
    stretch_ids = segment_ids.reshape(stretches, stretch_rows)
    prior_ids = before_ids.reshape(stretches, stretch_rows)[:, 0]
    ends_mask = (segment_ids != next_ids).reshape(stretches, stretch_rows)
    step_sizes = jax.nn.softplus(steps_sum + step_bias[None, :])
    decay_steps = step_sizes * decay_rate[None, :]
    log_decay = -jnp.cumsum(decay_steps.reshape(stretches, stretch_rows, local_heads), axis=1)
    decay_heads = jnp.swapaxes(log_decay, 1, 2)
    step_heads = jnp.swapaxes(step_sizes.reshape(stretches, stretch_rows, local_heads), 1, 2)
    values = head_values.reshape(stretches, stretch_rows, local_heads, head_width)
    write_state = both_states[:, :state_width].reshape(stretches, stretch_rows, state_width)
    read_state = both_states[:, state_width:].reshape(stretches, stretch_rows, state_width)
    intersection = jnp.einsum(
        "ctn,csn->cts", read_state, write_state, preferred_element_type=jnp.float32
    )
    token_order = jnp.arange(stretch_rows, dtype=jnp.int32)
    causal = token_order[:, None] >= token_order[None, :]
    allowed = causal[None] & (stretch_ids[:, :, None] == stretch_ids[:, None, :])
    spread = decay_heads[:, :, :, None] - decay_heads[:, :, None, :]
    weights = (
        jnp.where(allowed[:, None], jnp.exp(jnp.minimum(spread, 0.0)), 0.0)
        * step_heads[:, :, None, :]
    )
    scores = (intersection[:, None] * weights).astype(jnp.bfloat16)
    within_stretch = jnp.einsum(
        "chts,cshp->cthp", scores, values, preferred_element_type=jnp.float32
    )
    last_ids = stretch_ids[:, -1]
    tail_decay = decay_heads[:, :, -1:]
    keep_tail = (stretch_ids == last_ids[:, None])[:, None, :]
    tail_coef = (
        jnp.where(keep_tail, jnp.exp(jnp.minimum(tail_decay - decay_heads, 0.0)), 0.0) * step_heads
    )
    tail_rows = (values.astype(jnp.float32) * jnp.swapaxes(tail_coef, 1, 2)[:, :, :, None]).astype(
        jnp.bfloat16
    )
    stretch_states = jnp.einsum(
        "clhp,cln->chpn", tail_rows, write_state, preferred_element_type=jnp.float32
    )
    stretch_gates = (
        jnp.exp(decay_heads[:, :, -1]) * (last_ids == prior_ids).astype(jnp.float32)[:, None]
    )
    own_pair = (stretch_gates[0], stretch_states[0])
    g1, s1 = from_behind(own_pair, "seq", 1)
    g2, s2 = from_behind(own_pair, "seq", 2)
    g3, s3 = from_behind(own_pair, "seq", 3)
    incoming = s1 + g1[:, None, None] * (s2 + g2[:, None, None] * s3)
    arriving = incoming[None]
    carry_mask = (stretch_ids == prior_ids[:, None]).astype(jnp.float32)
    carry_decay = jnp.exp(log_decay) * carry_mask[:, :, None]
    from_before = (
        jnp.einsum(
            "cln,chpn->clhp",
            read_state,
            arriving.astype(jnp.bfloat16),
            preferred_element_type=jnp.float32,
        )
        * carry_decay[:, :, :, None]
    )
    result = (
        within_stretch + from_before + skip_gain[None, None, :, None] * values.astype(jnp.float32)
    )
    ssm_rows = result.reshape(block_rows, local_width).astype(jnp.bfloat16)
    end_weight = ends_mask.astype(jnp.float32)
    has_end = jnp.sum(end_weight, axis=1)
    end_decay = jnp.sum(decay_heads * end_weight[:, None, :], axis=2)
    end_ids = jnp.sum(jnp.where(ends_mask, stretch_ids, 0), axis=1)
    keep_end = ((stretch_ids == end_ids[:, None]) & (has_end[:, None] > 0))[:, None, :]
    end_coef = (
        jnp.where(keep_end, jnp.exp(jnp.minimum(end_decay[:, :, None] - decay_heads, 0.0)), 0.0)
        * step_heads
    )
    end_rows = (values.astype(jnp.float32) * jnp.swapaxes(end_coef, 1, 2)[:, :, :, None]).astype(
        jnp.bfloat16
    )
    end_states = jnp.einsum(
        "clhp,cln->chpn", end_rows, write_state, preferred_element_type=jnp.float32
    )
    end_carry = (
        jnp.exp(end_decay) * ((end_ids == prior_ids) & (has_end > 0)).astype(jnp.float32)[:, None]
    )
    end_states = end_states + end_carry[:, :, None, None] * arriving
    final_block = jnp.sum(end_states, axis=0)[None]
    head_gates = gates_sum.astype(jnp.bfloat16)
    both = jnp.stack([ssm_rows, head_gates]).reshape(2, groups, sub_rows, local_width)
    returned = lax.all_to_all(both, "head", split_axis=1, concat_axis=3, tiled=True)
    token_rows = returned.reshape(2, sub_rows, inner_width).astype(jnp.float32)
    gated = token_rows[0] * jax.nn.silu(token_rows[1])
    mean_square = jnp.mean(gated * gated, axis=1)
    scaled = gated * lax.rsqrt(mean_square + epsilon)[:, None] * norm_gain[None, :]
    gated_out = scaled.astype(jnp.bfloat16)
    return (gated_out, final_block)


def solution(mesh):
    in_specs = (
        P(("seq", "head"), None),
        P("seq", "head"),
        P("seq", "head"),
        P("seq", "head"),
        P("seq", None),
        P(),
        P(),
        P("head"),
        P("head"),
        P("head"),
        P(),
        P(),
    )
    out_specs = (P(("seq", "head"), None), P("seq", "head", None, None))
    return jax.shard_map(
        on_device, mesh=mesh, in_specs=in_specs, out_specs=out_specs, check_vma=False
    )
```

profile of v0, /device:TPU:5, one launch (start us, length us, event | category | flops | bytes accessed | tf_op | source)
XLA Modules:
  0.0 259.8 jit_solution(16076834221550302030)
XLA Ops:
  7.2 0.8 copy.65
  8.0 1.4 maximum_bitcast_fusion
  9.5 2.1 broadcast_in_dim.39
  11.6 4.3 %all-to-all-start = ((bf16[4,64,2560]{2,1,0:T(8,128)(2,1)}), bf16[4,64,2560]{2,1,0:T(8,128)(2,1)S(1)}, u32[]{:S(2)}, u32[]{:S(2)}) async-start(bf16[4,64,2560]{2,1,0:T(8,128)(2,1)} %broadcast_in_dim.39), calls=%async_computation | async-start | bytes 2621440 | tf_op jit(solution)/shard_map/all_to_all | solution.py:45
  16.2 0.7 slice.91
  16.9 0.8 dynamic_slice.6
  17.8 0.7 slice.136
  18.5 0.6 fusion.49
  20.3 0.5 slice.139
  22.2 0.6 convert_reduce_fusion.4
  23.5 0.6 select_reduce_fusion
  24.3 0.7 broadcast_compare_fusion
  25.1 139.3 %all-gather.3.cloned.1.call-done = bf16[128,20,1546]{2,1,0:T(8,128)(2,1)} async-done(((bf16[1,20,1546]{2,1,0:T(8,128)(2,1)}), bf16[128,20,1546]{2,1,0:T(8,128)(2,1)}) %all-gather.3.cloned.1.call-update) | async-done | bytes 7915536 | tf_op jit(solution)/shard_map/all_gather | solution.py:52
  164.5 13.7 %reshape.504 = bf16[2560,1546]{1,0:T(8,128)(2,1)} reshape(bf16[128,20,1546]{2,1,0:T(8,128)(2,1)} %all-gather.3.cloned.1.call-done) | data formatting | bytes 15831040
  178.2 5.8 %fusion.50 = (bf16[256,1546]{0,1:T(8,128)(2,1)S(1)}, f32[256,1546]{0,1:T(8,128)S(1)}) fusion(bf16[2560,1546]{1,0:T(8,128)(2,1)} %reshape.504, bf16[256,2560]{1,0:T(8,128)(2,1)S(1)} %bitcast.126), kind=kOutput, calls=%fused_computation.113 | convolution fusion | flops 2026768896 | bytes 11600896 | tf_op jit(solution)/shard_map/dot_general | solution.py:53
  184.2 1.0 copy-done.4
  185.2 0.6 reduce-window.19
  186.2 0.2 multiply_reduce_fusion.1
  186.4 0.8 fusion.31
  187.4 3.4 %collective-permute-start.4 = (f32[10]{0:T(128)S(1)}, f32[10]{0:T(128)S(1)}, u32[]{:S(2)}, u32[]{:S(2)}) collective-permute-start(f32[10]{0:T(128)S(1)} %exponential_multiply_fusion.1), channel_id=1, source_target_pairs={{0,8},{4,12},{8,16},{12,20},{16,24},{20,28},{24,32},{28,36},{32,40... | collective-permute-start | bytes 128 | tf_op jit(solution)/shard_map/ppermute | solution.py:13
  190.8 2.8 %collective-permute-start.2 = (f32[10]{0:T(128)S(1)}, f32[10]{0:T(128)S(1)}, u32[]{:S(2)}, u32[]{:S(2)}) collective-permute-start(f32[10]{0:T(128)S(1)} %exponential_multiply_fusion.1), channel_id=1, source_target_pairs={{0,4},{4,8},{8,12},{12,16},{16,20},{20,24},{24,28},{28,32},{32,36}... | collective-permute-start | bytes 128 | tf_op jit(solution)/shard_map/ppermute | solution.py:13
  193.8 1.9 collective-permute-start
  195.8 0.8 fusion.32
  196.7 0.2 copy.74
  196.9 0.8 copy.75
  197.7 0.9 collective-permute-done
  198.7 1.5 multiply_convert_fusion.4
  200.2 0.8 fusion.12
  201.1 0.2 fusion.20
  201.3 4.4 %collective-permute-start.1 = (f32[10,64,128]{2,1,0:T(8,128)S(1)}, f32[10,64,128]{2,1,0:T(8,128)S(1)}, u32[]{:S(2)}, u32[]{:S(2)}) collective-permute-start(f32[10,64,128]{2,1,0:T(8,128)S(1)} %fusion.20), channel_id=1, source_target_pairs={{0,4},{4,8},{8,12},{12,16},{16,20},{20,24},{24,28},{28,32},{32,36}... | collective-permute-start | bytes 983048 | tf_op jit(solution)/shard_map/ppermute | solution.py:13
  205.7 3.0 %collective-permute-start.3 = (f32[10,64,128]{2,1,0:T(8,128)S(1)}, f32[10,64,128]{2,1,0:T(8,128)S(1)}, u32[]{:S(2)}, u32[]{:S(2)}) collective-permute-start(f32[10,64,128]{2,1,0:T(8,128)S(1)} %fusion.20), channel_id=1, source_target_pairs={{0,8},{4,12},{8,16},{12,20},{16,24},{20,28},{24,32},{28,36},{32,40... | collective-permute-start | bytes 983048 | tf_op jit(solution)/shard_map/ppermute | solution.py:13
  208.7 2.5 collective-permute-start.5
  211.2 0.2 fusion.26
  211.4 0.9 fusion.7
  212.4 11.8 %collective-permute-done.3 = f32[10,64,128]{2,1,0:T(8,128)S(1)} collective-permute-done((f32[10,64,128]{2,1,0:T(8,128)S(1)}, f32[10,64,128]{2,1,0:T(8,128)S(1)}, u32[]{:S(2)}, u32[]{:S(2)}) %collective-permute-start.3) | collective-permute-done | bytes 327712 | tf_op jit(solution)/shard_map/ppermute | solution.py:13
  224.2 7.7 %collective-permute-done.5 = f32[10,64,128]{2,1,0:T(8,128)S(1)} collective-permute-done((f32[10,64,128]{2,1,0:T(8,128)S(1)}, f32[10,64,128]{2,1,0:T(8,128)S(1)}, u32[]{:S(2)}, u32[]{:S(2)}) %collective-permute-start.5) | collective-permute-done | bytes 327712 | tf_op jit(solution)/shard_map/ppermute | solution.py:13
  232.1 0.2 fusion.11
  232.3 0.3 convert_element_type.165
  232.6 1.1 pad_maximum_fusion
  233.7 2.4 copy.76
  236.1 4.0 %all-to-all-start.1 = ((bf16[2,4,64,640]{3,2,0,1:T(8,128)(2,1)}), bf16[2,4,64,640]{3,2,0,1:T(8,128)(2,1)S(1)}, u32[]{:S(2)}, u32[]{:S(2)}) async-start(bf16[2,4,64,640]{3,2,0,1:T(8,128)(2,1)} %copy.76), calls=%async_computation.1 | async-start | bytes 1310720 | tf_op jit(solution)/shard_map/all_to_all | solution.py:183
  240.8 1.0 add_bitcast_fusion
  241.8 8.4 %all-to-all-done.1 = bf16[2,4,64,640]{3,2,0,1:T(8,128)(2,1)S(1)} async-done(((bf16[2,4,64,640]{3,2,0,1:T(8,128)(2,1)}), bf16[2,4,64,640]{3,2,0,1:T(8,128)(2,1)S(1)}, u32[]{:S(2)}, u32[]{:S(2)}) %all-to-all-start.1) | async-done | bytes 655392 | tf_op jit(solution)/shard_map/all_to_all | solution.py:183
  250.4 0.4 copy.77
  250.9 0.4 copy.78
  251.4 0.3 multiply_reduce_fusion
  251.8 0.3 copy-done.2
  252.1 0.8 multiply_convert_fusion.5
  (68 shorter events, 2.3 us)
Async XLA Ops:
  7.2 157.3 %all-gather.3.cloned.1.call-start = ((), (), s32[]{:S(2)}) async-start(), calls=%async_computation.2 | async-start | bytes 10303488 | tf_op jit(solution)/shard_map/all_gather | solution.py:52
  11.6 4.3 %copy-start.5 = (s32[64]{0:T(128)S(1)}, s32[64]{0:T(128)}, u32[]{:S(2)}) copy-start(s32[64]{0:T(128)} %param.23) | copy-start | bytes 772
  11.6 11.8 %copy-start.1 = (f32[4,2816]{1,0:T(4,128)S(1)}, f32[4,2816]{1,0:T(4,128)}, u32[]{:S(2)}) copy-start(f32[4,2816]{1,0:T(4,128)} %param.17) | copy-start | bytes 135172
  11.6 11.8 %slice-start = ((f32[4,2816]{1,0:T(4,128)}), f32[4,256]{1,0:T(4,128)S(1)}, s32[]{:S(2)}) async-start(f32[4,2816]{1,0:T(4,128)} %param.17), calls=%async_computation.3 | async-start | bytes 8192 | tf_op jit(solution)/shard_map/slice | solution.py:61
  11.6 166.6 %all-to-all-start = ((bf16[4,64,2560]{2,1,0:T(8,128)(2,1)}), bf16[4,64,2560]{2,1,0:T(8,128)(2,1)S(1)}, u32[]{:S(2)}, u32[]{:S(2)}) async-start(bf16[4,64,2560]{2,1,0:T(8,128)(2,1)} %broadcast_in_dim.39), calls=%async_computation | async-start | bytes 2621440 | tf_op jit(solution)/shard_map/all_to_all | solution.py:45
  178.2 5.9 %copy-start.3 = (f32[10]{0:T(128)S(1)}, f32[10]{0:T(128)}, u32[]{:S(2)}) copy-start(f32[10]{0:T(128)} %param.19) | copy-start | bytes 124
  178.2 5.9 %copy-start.6 = (f32[10]{0:T(128)S(1)}, f32[10]{0:T(128)}, u32[]{:S(2)}) copy-start(f32[10]{0:T(128)} %param.20) | copy-start | bytes 124
  184.0 1.2 copy-start.4
  187.4 24.9 %collective-permute-start.4 = (f32[10]{0:T(128)S(1)}, f32[10]{0:T(128)S(1)}, u32[]{:S(2)}, u32[]{:S(2)}) collective-permute-start(f32[10]{0:T(128)S(1)} %exponential_multiply_fusion.1), channel_id=1, source_target_pairs={{0,8},{4,12},{8,16},{12,20},{16,24},{20,28},{24,32},{28,36},{32,40... | collective-permute-start | bytes 128 | tf_op jit(solution)/shard_map/ppermute | solution.py:13
  190.8 21.5 %collective-permute-start.2 = (f32[10]{0:T(128)S(1)}, f32[10]{0:T(128)S(1)}, u32[]{:S(2)}, u32[]{:S(2)}) collective-permute-start(f32[10]{0:T(128)S(1)} %exponential_multiply_fusion.1), channel_id=1, source_target_pairs={{0,4},{4,8},{8,12},{12,16},{16,20},{20,24},{24,28},{28,32},{32,36}... | collective-permute-start | bytes 128 | tf_op jit(solution)/shard_map/ppermute | solution.py:13
  193.8 4.9 %collective-permute-start = (bf16[3,896]{0,1:T(8,128)(2,1)S(1)}, bf16[3,896]{0,1:T(8,128)(2,1)S(1)}, u32[]{:S(2)}, u32[]{:S(2)}) collective-permute-start(bf16[3,896]{0,1:T(8,128)(2,1)S(1)} %slice.120), channel_id=1, source_target_pairs={{0,4},{4,8},{8,12},{12,16},{16,20},{20,24},{24,28},{28,32},{32,36}... | collective-permute-start | bytes 16136 | tf_op jit(solution)/shard_map/ppermute | solution.py:13
  201.3 11.0 %collective-permute-start.1 = (f32[10,64,128]{2,1,0:T(8,128)S(1)}, f32[10,64,128]{2,1,0:T(8,128)S(1)}, u32[]{:S(2)}, u32[]{:S(2)}) collective-permute-start(f32[10,64,128]{2,1,0:T(8,128)S(1)} %fusion.20), channel_id=1, source_target_pairs={{0,4},{4,8},{8,12},{12,16},{16,20},{20,24},{24,28},{28,32},{32,36}... | collective-permute-start | bytes 983048 | tf_op jit(solution)/shard_map/ppermute | solution.py:13
  205.7 18.5 %collective-permute-start.3 = (f32[10,64,128]{2,1,0:T(8,128)S(1)}, f32[10,64,128]{2,1,0:T(8,128)S(1)}, u32[]{:S(2)}, u32[]{:S(2)}) collective-permute-start(f32[10,64,128]{2,1,0:T(8,128)S(1)} %fusion.20), channel_id=1, source_target_pairs={{0,8},{4,12},{8,16},{12,20},{16,24},{20,28},{24,32},{28,36},{32,40... | collective-permute-start | bytes 983048 | tf_op jit(solution)/shard_map/ppermute | solution.py:13
  208.7 23.2 %collective-permute-start.5 = (f32[10,64,128]{2,1,0:T(8,128)S(1)}, f32[10,64,128]{2,1,0:T(8,128)S(1)}, u32[]{:S(2)}, u32[]{:S(2)}) collective-permute-start(f32[10,64,128]{2,1,0:T(8,128)S(1)} %fusion.20), channel_id=1, source_target_pairs={{0,12},{4,16},{8,20},{12,24},{16,28},{20,32},{24,36},{28,40},{32,4... | collective-permute-start | bytes 983048 | tf_op jit(solution)/shard_map/ppermute | solution.py:13
  211.4 20.7 %copy-start.7 = (f32[10]{0:T(128)S(1)}, f32[10]{0:T(128)}, u32[]{:S(2)}) copy-start(f32[10]{0:T(128)} %param.21) | copy-start | bytes 124
  233.7 7.1 %copy-start = (bf16[256,640]{0,1:T(8,128)(2,1)S(1)}, bf16[256,640]{0,1:T(8,128)(2,1)}, u32[]{:S(2)}) copy-start(bf16[256,640]{0,1:T(8,128)(2,1)} %get-tuple-element.20) | copy-start | bytes 983044
  236.1 14.1 %all-to-all-start.1 = ((bf16[2,4,64,640]{3,2,0,1:T(8,128)(2,1)}), bf16[2,4,64,640]{3,2,0,1:T(8,128)(2,1)S(1)}, u32[]{:S(2)}, u32[]{:S(2)}) async-start(bf16[2,4,64,640]{3,2,0,1:T(8,128)(2,1)} %copy.76), calls=%async_computation.1 | async-start | bytes 1310720 | tf_op jit(solution)/shard_map/all_to_all | solution.py:183
  251.4 0.7 copy-start.2
Sparse Core Ops, SparseCore 0:
  11.7 152.7 all-gather.2
where the time goes:
time: 261 us; the launch traced here: 260 us
  waiting for transfers between devices  168 us (64%)
  local copies, waits for them, and re-layouts  26.9 us (10%)
  starting transfers between devices  26.3 us (10%)
  between operations  18.4 us (7%)
  other arithmetic  11.4 us (4%)
  matrix products  8.44 us (3%)
    all_gather x1, waiting for transfers between devices, on_device(): full = lax.all_gather(merged, 'seq', axis=0, tiled=True)  139 us
    ppermute x6, waiting for transfers between devices, from_behind(): return lax.ppermute(block, axis, route)  20.5 us
    ppermute x6, starting transfers between devices, from_behind(): return lax.ppermute(block, axis, route)  18 us
    unnamed x24, local copies, waits for them, and re-layouts  16 us
    all_to_all x1, waiting for transfers between devices, on_device(): lax.all_to_all(both, 'head', split_axis=1, concat_axis=3, tiled=True)  8.45 us
    dot_general x1, matrix products, on_device(): projected = jnp.dot(block_hidden, full, preferred_element_type=jnp.float32)  5.84 us
  transfers between devices with their start and end apart: 9, of which 5 were waited for; matrix products, arithmetic and copies ran while one was open for 11% of the time, Pallas kernels for 0%

commit v1 on v0

--- a/solution.py
+++ b/solution.py
@@ -49,7 +49,10 @@
     sub_rows = block_rows // groups
     step_width = w_steps.shape[1]
     merged = jnp.concatenate([w_values, w_states, w_gates, w_steps], axis=1)
-    full = lax.all_gather(merged, "seq", axis=0, tiled=True)
+    size = lax.axis_size("seq")
+    parts = jnp.stack([merged for _ in range(size)])
+    parts = lax.all_to_all(parts, "seq", split_axis=0, concat_axis=0)
+    full = jnp.concatenate(parts, axis=0)
     projected = jnp.dot(block_hidden, full, preferred_element_type=jnp.float32)
     conv_end = local_width + 2 * state_width
     pre_rows = projected[:, :conv_end].astype(jnp.bfloat16)

time: 261 us -> 569 us (2.18)
  the two profiles are of different devices: /device:TPU:5 before, /device:TPU:3 now
where the time goes in v1:
time: 569 us; the launch traced here: 568 us
  waiting for transfers between devices  460 us (81%)
  starting transfers between devices  53 us (9%)
  local copies, waits for them, and re-layouts  30.5 us (5%)
  other arithmetic  10.8 us (2%)
  matrix products  8.43 us (1%)
    all_to_all x1, waiting for transfers between devices, on_device(): parts = lax.all_to_all(parts, 'seq', split_axis=0, concat_axis=0)  433 us
    ppermute x6, starting transfers between devices, from_behind(): return lax.ppermute(block, axis, route)  25 us
    all_to_all x1, starting transfers between devices, on_device(): parts = lax.all_to_all(parts, 'seq', split_axis=0, concat_axis=0)  20.4 us
    ppermute x6, waiting for transfers between devices, from_behind(): return lax.ppermute(block, axis, route)  19.1 us
    reshape x1, local copies, waits for them, and re-layouts, on_device(): full = jnp.concatenate(parts, axis=0)  13.7 us
  transfers between devices with their start and end apart: 9, of which 5 were waited for; matrix products, arithmetic and copies ran while one was open for 5% of the time, Pallas kernels for 0%

profile of v1, /device:TPU:3, one launch (start us, length us, event | category | flops | bytes accessed | tf_op | source)
XLA Modules:
  0.0 568.1 jit_solution(8997134225011356284)
XLA Ops:
  0.6 0.8 copy.65
  1.4 0.8 pad_maximum_fusion.2
  2.2 4.5 stack.6
  6.8 20.4 %all-to-all-start = ((bf16[128,20,1546]{2,1,0:T(8,128)(2,1)}), bf16[128,20,1546]{2,1,0:T(8,128)(2,1)}, u32[]{:S(2)}, u32[]{:S(2)}) async-start(bf16[128,20,1546]{2,1,0:T(8,128)(2,1)} %stack.6), calls=%async_computation | async-start | bytes 20447232 | tf_op jit(solution)/shard_map/all_to_all | solution.py:54
  27.5 0.7 slice.91
  28.2 0.8 dynamic_slice.6
  29.0 0.7 slice.136
  29.7 0.6 fusion.49
  31.6 0.5 slice.139
  33.5 0.6 convert_reduce_fusion.4
  34.8 0.6 select_reduce_fusion
  35.6 433.5 %all-to-all-done = bf16[128,20,1546]{2,1,0:T(8,128)(2,1)} async-done(((bf16[128,20,1546]{2,1,0:T(8,128)(2,1)}), bf16[128,20,1546]{2,1,0:T(8,128)(2,1)}, u32[]{:S(2)}, u32[]{:S(2)}) %all-to-all-start) | async-done | bytes 7915552 | tf_op jit(solution)/shard_map/all_to_all | solution.py:54
  469.1 1.2 broadcast_in_dim.39
  470.2 4.2 all-to-all-start.1
  474.4 0.6 broadcast_compare_fusion
  475.3 13.7 %reshape.491 = bf16[2560,1546]{1,0:T(8,128)(2,1)} reshape(bf16[128,20,1546]{2,1,0:T(8,128)(2,1)} %all-to-all-done) | data formatting | bytes 15831040 | tf_op jit(solution)/shard_map/reshape | solution.py:55
  489.0 5.8 %fusion.50 = (bf16[256,1546]{0,1:T(8,128)(2,1)S(1)}, f32[256,1546]{0,1:T(8,128)S(1)}) fusion(bf16[2560,1546]{1,0:T(8,128)(2,1)} %reshape.491, bf16[256,2560]{1,0:T(8,128)(2,1)S(1)} %bitcast.124), kind=kOutput, calls=%fused_computation.113 | convolution fusion | flops 2026768896 | bytes 11600896 | tf_op jit(solution)/shard_map/dot_general | solution.py:56
  495.0 1.0 copy-done.5
  496.0 0.6 reduce-window.19
  497.2 0.8 fusion.31
  498.2 6.7 %collective-permute-start.4 = (f32[10]{0:T(128)S(1)}, f32[10]{0:T(128)S(1)}, u32[]{:S(2)}, u32[]{:S(2)}) collective-permute-start(f32[10]{0:T(128)S(1)} %exponential_multiply_fusion.1), channel_id=1, source_target_pairs={{0,8},{4,12},{8,16},{12,20},{16,24},{20,28},{24,32},{28,36},{32,40... | collective-permute-start | bytes 128 | tf_op jit(solution)/shard_map/ppermute | solution.py:13
  504.9 4.3 collective-permute-start.2
  509.4 1.9 collective-permute-start
  511.4 0.8 fusion.32
  512.3 0.2 copy.74
  512.5 0.8 copy.75
  513.3 0.9 collective-permute-done
  514.3 1.5 multiply_convert_fusion.4
  515.9 0.8 fusion.12
  516.7 0.2 fusion.20
  516.9 4.9 collective-permute-start.1
  521.9 4.9 collective-permute-start.3
  526.8 2.2 collective-permute-start.5
  529.2 0.9 fusion.7
  530.2 11.2 %collective-permute-done.3 = f32[10,64,128]{2,1,0:T(8,128)S(1)} collective-permute-done((f32[10,64,128]{2,1,0:T(8,128)S(1)}, f32[10,64,128]{2,1,0:T(8,128)S(1)}, u32[]{:S(2)}, u32[]{:S(2)}) %collective-permute-start.3) | collective-permute-done | bytes 327712 | tf_op jit(solution)/shard_map/ppermute | solution.py:13
  541.4 7.0 %collective-permute-done.5 = f32[10,64,128]{2,1,0:T(8,128)S(1)} collective-permute-done((f32[10,64,128]{2,1,0:T(8,128)S(1)}, f32[10,64,128]{2,1,0:T(8,128)S(1)}, u32[]{:S(2)}, u32[]{:S(2)}) %collective-permute-start.5) | collective-permute-done | bytes 327712 | tf_op jit(solution)/shard_map/ppermute | solution.py:13
  548.5 0.2 fusion.11
  548.7 0.3 convert_element_type.165
  549.0 1.1 pad_maximum_fusion
  550.1 2.4 copy.76
  552.5 3.5 all-to-all-start.2
  556.6 1.0 add_bitcast_fusion
  557.6 7.8 %all-to-all-done.2 = bf16[2,4,64,640]{3,2,0,1:T(8,128)(2,1)S(1)} async-done(((bf16[2,4,64,640]{3,2,0,1:T(8,128)(2,1)}), bf16[2,4,64,640]{3,2,0,1:T(8,128)(2,1)S(1)}, u32[]{:S(2)}, u32[]{:S(2)}) %all-to-all-start.2) | async-done | bytes 655392 | tf_op jit(solution)/shard_map/all_to_all | solution.py:186
  565.6 0.4 copy.77
  566.1 0.4 copy.78
  566.6 0.3 multiply_reduce_fusion
  566.9 0.3 copy-done.3
  567.2 0.8 multiply_convert_fusion.5
  (70 shorter events, 2.6 us)
Async XLA Ops:
  6.7 20.4 %copy-start.6 = (s32[64]{0:T(128)S(1)}, s32[64]{0:T(128)}, u32[]{:S(2)}) copy-start(s32[64]{0:T(128)} %param.23) | copy-start | bytes 772
  6.7 28.0 %copy-start.2 = (f32[4,2816]{1,0:T(4,128)S(1)}, f32[4,2816]{1,0:T(4,128)}, u32[]{:S(2)}) copy-start(f32[4,2816]{1,0:T(4,128)} %param.17) | copy-start | bytes 135172
  6.7 28.0 %slice-start = ((f32[4,2816]{1,0:T(4,128)}), f32[4,256]{1,0:T(4,128)S(1)}, s32[]{:S(2)}) async-start(f32[4,2816]{1,0:T(4,128)} %param.17), calls=%async_computation.3 | async-start | bytes 8192 | tf_op jit(solution)/shard_map/slice | solution.py:64
  6.7 462.3 %copy-start.1 = (bf16[64,2560]{1,0:T(8,128)(2,1)S(1)}, bf16[64,2560]{1,0:T(8,128)(2,1)}, u32[]{:S(2)}) copy-start(bf16[64,2560]{1,0:T(8,128)(2,1)} %param.12) | copy-start | bytes 983044
  6.8 462.3 %all-to-all-start = ((bf16[128,20,1546]{2,1,0:T(8,128)(2,1)}), bf16[128,20,1546]{2,1,0:T(8,128)(2,1)}, u32[]{:S(2)}, u32[]{:S(2)}) async-start(bf16[128,20,1546]{2,1,0:T(8,128)(2,1)} %stack.6), calls=%async_computation | async-start | bytes 20447232 | tf_op jit(solution)/shard_map/all_to_all | solution.py:54
  470.2 18.8 %all-to-all-start.1 = ((bf16[4,64,2560]{2,1,0:T(8,128)(2,1)}), bf16[4,64,2560]{2,1,0:T(8,128)(2,1)S(1)}, u32[]{:S(2)}, u32[]{:S(2)}) async-start(bf16[4,64,2560]{2,1,0:T(8,128)(2,1)} %broadcast_in_dim.39), calls=%async_computation.1 | async-start | bytes 2621440 | tf_op jit(solution)/shard_map/all_to_all | solution.py:45
  489.0 5.9 %copy-start.4 = (f32[10]{0:T(128)S(1)}, f32[10]{0:T(128)}, u32[]{:S(2)}) copy-start(f32[10]{0:T(128)} %param.19) | copy-start | bytes 124
  489.0 5.9 %copy-start.7 = (f32[10]{0:T(128)S(1)}, f32[10]{0:T(128)}, u32[]{:S(2)}) copy-start(f32[10]{0:T(128)} %param.20) | copy-start | bytes 124
  494.8 1.2 copy-start.5
  498.2 31.9 %collective-permute-start.4 = (f32[10]{0:T(128)S(1)}, f32[10]{0:T(128)S(1)}, u32[]{:S(2)}, u32[]{:S(2)}) collective-permute-start(f32[10]{0:T(128)S(1)} %exponential_multiply_fusion.1), channel_id=1, source_target_pairs={{0,8},{4,12},{8,16},{12,20},{16,24},{20,28},{24,32},{28,36},{32,40... | collective-permute-start | bytes 128 | tf_op jit(solution)/shard_map/ppermute | solution.py:13
  504.9 25.2 %collective-permute-start.2 = (f32[10]{0:T(128)S(1)}, f32[10]{0:T(128)S(1)}, u32[]{:S(2)}, u32[]{:S(2)}) collective-permute-start(f32[10]{0:T(128)S(1)} %exponential_multiply_fusion.1), channel_id=1, source_target_pairs={{0,4},{4,8},{8,12},{12,16},{16,20},{20,24},{24,28},{28,32},{32,36}... | collective-permute-start | bytes 128 | tf_op jit(solution)/shard_map/ppermute | solution.py:13
  509.4 4.9 collective-permute-start
  516.9 13.2 %collective-permute-start.1 = (f32[10,64,128]{2,1,0:T(8,128)S(1)}, f32[10,64,128]{2,1,0:T(8,128)S(1)}, u32[]{:S(2)}, u32[]{:S(2)}) collective-permute-start(f32[10,64,128]{2,1,0:T(8,128)S(1)} %fusion.20), channel_id=1, source_target_pairs={{0,4},{4,8},{8,12},{12,16},{16,20},{20,24},{24,28},{28,32},{32,36}... | collective-permute-start | bytes 983048 | tf_op jit(solution)/shard_map/ppermute | solution.py:13
  521.9 19.5 %collective-permute-start.3 = (f32[10,64,128]{2,1,0:T(8,128)S(1)}, f32[10,64,128]{2,1,0:T(8,128)S(1)}, u32[]{:S(2)}, u32[]{:S(2)}) collective-permute-start(f32[10,64,128]{2,1,0:T(8,128)S(1)} %fusion.20), channel_id=1, source_target_pairs={{0,8},{4,12},{8,16},{12,20},{16,24},{20,28},{24,32},{28,36},{32,40... | collective-permute-start | bytes 983048 | tf_op jit(solution)/shard_map/ppermute | solution.py:13
  526.8 21.5 %collective-permute-start.5 = (f32[10,64,128]{2,1,0:T(8,128)S(1)}, f32[10,64,128]{2,1,0:T(8,128)S(1)}, u32[]{:S(2)}, u32[]{:S(2)}) collective-permute-start(f32[10,64,128]{2,1,0:T(8,128)S(1)} %fusion.20), channel_id=1, source_target_pairs={{0,12},{4,16},{8,20},{12,24},{16,28},{20,32},{24,36},{28,40},{32,4... | collective-permute-start | bytes 983048 | tf_op jit(solution)/shard_map/ppermute | solution.py:13
  529.2 19.2 %copy-start.8 = (f32[10]{0:T(128)S(1)}, f32[10]{0:T(128)}, u32[]{:S(2)}) copy-start(f32[10]{0:T(128)} %param.21) | copy-start | bytes 124
  550.1 6.5 %copy-start = (bf16[256,640]{0,1:T(8,128)(2,1)S(1)}, bf16[256,640]{0,1:T(8,128)(2,1)}, u32[]{:S(2)}) copy-start(bf16[256,640]{0,1:T(8,128)(2,1)} %get-tuple-element.20) | copy-start | bytes 983044
  552.5 12.9 %all-to-all-start.2 = ((bf16[2,4,64,640]{3,2,0,1:T(8,128)(2,1)}), bf16[2,4,64,640]{3,2,0,1:T(8,128)(2,1)S(1)}, u32[]{:S(2)}, u32[]{:S(2)}) async-start(bf16[2,4,64,640]{3,2,0,1:T(8,128)(2,1)} %copy.76), calls=%async_computation.2 | async-start | bytes 1310720 | tf_op jit(solution)/shard_map/all_to_all | solution.py:186
  566.5 0.7 copy-start.3
